TPU v7x, 32 devices: a whole 2x2x4 slice. The times are simulated.
32 devices in a mesh: row: 8 (over y, x, core), col: 4 (over z).
Axes of the slice: x: 2, y: 2, z: 4, core: 2. Of those that a mesh axis runs over, the one named last changes fastest.
Arguments:
- tokens: bfloat16 [192, 8192], P('col', 'row'), may hold values from -6 to 6
- grad_out: bfloat16 [192, 8192], P('col', 'row'), may hold values from -6 to 6
- gate_weight: bfloat16 [8192, 14336], P('row', 'col'), may hold values from -0.0625 to 0.0625
- up_weight: bfloat16 [8192, 14336], P('row', 'col'), may hold values from -0.0625 to 0.0625
- down_weight: bfloat16 [14336, 8192], P('col', 'row'), may hold values from -0.046875 to 0.046875
Outputs:
- grad_tokens: bfloat16 [192, 8192], P('col', 'row')
- grad_gate_weight: bfloat16 [8192, 14336], P('row', 'col')
- grad_up_weight: bfloat16 [8192, 14336], P('row', 'col')
- grad_down_weight: bfloat16 [14336, 8192], P('col', 'row')
All inputs are finite; a program needn't handle non-finite values.
Results may differ from a plain program's by a relative error of at most 0.024.
Values may be sent and summed in bfloat16 or wider, within the bound.
No kernel may reach another device: no remote copies, remote signals or barrier semaphores. Data moves between devices by JAX's collectives and lax.ppermute only.
A program may use at most 128 MiB of HBM per device.

v0:
```python
import jax
import jax.numpy as jnp
from jax import lax
from jax.sharding import PartitionSpec as P


def contract_first(left, right):
    return lax.dot_general(
        left, right, (((0,), (0,)), ((), ())), preferred_element_type=jnp.float32
    )


def contract_last(left, right):
    return lax.dot_general(
        left, right, (((1,), (1,)), ((), ())), preferred_element_type=jnp.float32
    )


def gated_grads(gate_sum, up_sum, grad_hidden):
    sigmoid_gate = jax.nn.sigmoid(gate_sum)
    hidden = (gate_sum * sigmoid_gate * up_sum).astype(jnp.bfloat16)
    grad_up = (grad_hidden * gate_sum * sigmoid_gate).astype(jnp.bfloat16)
    grad_gate = (
        grad_hidden * up_sum * sigmoid_gate * (1.0 + gate_sum * (1.0 - sigmoid_gate))
    ).astype(jnp.bfloat16)
    return (hidden, grad_gate, grad_up)


def pick_chunks(units, wanted):
    for n in range(wanted, 0, -1):
        if units % n == 0 and units // n % 128 == 0:
            return n
    return 1


N_CHUNKS = 2


def body(tokens, grad_out, gate_weight, up_weight, down_weight):
    feat = tokens.shape[1]
    both = jnp.concatenate([tokens, grad_out], axis=1)
    both_all = lax.all_gather(both, "col", axis=0, tiled=True)
    tok_all = both_all[:, :feat]
    grad_all = both_all[:, feat:]
    tok_t = tok_all.T
    units = gate_weight.shape[1]
    n_chunks = pick_chunks(units, N_CHUNKS)
    span = units // n_chunks
    acc_gate, acc_up, acc_down = ([], [], [])
    partial_grad = None
    prev = None
    for k in range(n_chunks):
        lo = k * span
        gw = gate_weight[:, lo : lo + span]
        uw = up_weight[:, lo : lo + span]
        dw = down_weight[lo : lo + span, :]
        parts = (
            jnp.dot(tok_all, gw, preferred_element_type=jnp.float32).astype(jnp.bfloat16),
            jnp.dot(tok_all, uw, preferred_element_type=jnp.float32).astype(jnp.bfloat16),
            contract_last(grad_all, dw).astype(jnp.bfloat16),
        )
        if prev is not None:
            parts, _ = lax.optimization_barrier((parts, prev))
        sums = lax.psum(parts, "row")
        prev = sums
        gate_sum, up_sum, grad_hidden = (s.astype(jnp.float32) for s in sums)
        hidden, grad_gate, grad_up = gated_grads(gate_sum, up_sum, grad_hidden)
        acc_gate.append(
            jnp.dot(tok_t, grad_gate, preferred_element_type=jnp.float32).astype(jnp.bfloat16)
        )
        acc_up.append(
            jnp.dot(tok_t, grad_up, preferred_element_type=jnp.float32).astype(jnp.bfloat16)
        )
        acc_down.append(contract_first(hidden, grad_all).astype(jnp.bfloat16))
        part = contract_last(grad_gate, gw) + contract_last(grad_up, uw)
        partial_grad = part if partial_grad is None else partial_grad + part
    grad_tokens = lax.psum_scatter(
        partial_grad.astype(jnp.bfloat16), "col", scatter_dimension=0, tiled=True
    )
    return (
        grad_tokens,
        jnp.concatenate(acc_gate, axis=1),
        jnp.concatenate(acc_up, axis=1),
        jnp.concatenate(acc_down, axis=0),
    )


def solution(mesh):
    return jax.shard_map(
        body,
        mesh=mesh,
        in_specs=(
            P("col", "row"),
            P("col", "row"),
            P("row", "col"),
            P("row", "col"),
            P("col", "row"),
        ),
        out_specs=(P("col", "row"), P("row", "col"), P("row", "col"), P("col", "row")),
        check_vma=False,
    )
```

profile of v0, /device:TPU:0, one launch (start us, length us, event | category | flops | bytes accessed | tf_op | source)
XLA Modules:
  0.0 214.4 jit_solution(11317851768424443296)
XLA Ops:
  7.2 1.0 pad_maximum_fusion.3
  8.2 21.4 %all_gather.3 = bf16[192,2048]{1,0:T(8,128)(2,1)S(1)} all-gather(bf16[48,2048]{1,0:T(8,128)(2,1)S(1)} %pad_maximum_fusion.3), channel_id=1, replica_groups=mesh['row'=8,'col'=4] {'col'}, dimensions={0}, use_global_device_ids=true | all-gather | bytes 983040 | tf_op jit(solution)/shard_map/all_gather | solution.py:42
  29.6 3.9 %fusion.23 = bf16[192,1792]{1,0:T(8,128)(2,1)} fusion(bf16[1024,3584]{1,0:T(8,128)(2,1)} %param.7, bf16[192,2048]{1,0:T(8,128)(2,1)S(1)} %all_gather.3), kind=kOutput, calls=%fused_computation.30 | convolution fusion | flops 704987136 | bytes 4751360 | tf_op jit(solution)/shard_map/dot_general | solution.py:58
  33.5 3.8 %fusion.20 = bf16[192,1792]{1,0:T(8,128)(2,1)} fusion(bf16[1024,3584]{1,0:T(8,128)(2,1)} %param.8, bf16[192,2048]{1,0:T(8,128)(2,1)S(1)} %all_gather.3), kind=kOutput, calls=%fused_computation.29 | convolution fusion | flops 704987136 | bytes 4751360 | tf_op jit(solution)/shard_map/dot_general | solution.py:59
  37.3 2.2 %fusion.32 = bf16[192,1792]{1,0:T(8,128)(2,1)} fusion(bf16[3584,1024]{1,0:T(8,128)(2,1)S(1)} %bitcast.1, bf16[192,2048]{1,0:T(8,128)(2,1)S(1)} %all_gather.3), kind=kOutput, calls=%fused_computation.33 | convolution fusion | flops 704987136 | bytes 4751360 | tf_op jit(solution)/shard_map/dot_general | solution.py:14
  39.6 3.8 %fusion.26 = bf16[192,1792]{1,0:T(8,128)(2,1)} fusion(bf16[1024,3584]{1,0:T(8,128)(2,1)} %param.7, bf16[192,2048]{1,0:T(8,128)(2,1)S(1)} %all_gather.3), kind=kOutput, calls=%fused_computation.31 | convolution fusion | flops 704987136 | bytes 4751360 | tf_op jit(solution)/shard_map/dot_general | solution.py:58
  43.4 4.2 %fusion.29 = bf16[192,1792]{1,0:T(8,128)(2,1)} fusion(bf16[1024,3584]{1,0:T(8,128)(2,1)} %param.8, bf16[192,2048]{1,0:T(8,128)(2,1)S(1)} %all_gather.3), kind=kOutput, calls=%fused_computation.32 | convolution fusion | flops 704987136 | bytes 4751360 | tf_op jit(solution)/shard_map/dot_general | solution.py:59
  47.6 4.3 %fusion.35 = bf16[192,1792]{1,0:T(8,128)(2,1)} fusion(bf16[3584,1024]{1,0:T(8,128)(2,1)} %param.9, bf16[192,2048]{1,0:T(8,128)(2,1)S(1)} %all_gather.3), kind=kOutput, calls=%fused_computation.34 | convolution fusion | flops 704987136 | bytes 4751360 | tf_op jit(solution)/shard_map/dot_general | solution.py:14
  51.9 49.2 %all-reduce.7.cloned.1.call-done = (bf16[192,1792]{1,0:T(8,128)(2,1)}, bf16[192,1792]{1,0:T(8,128)(2,1)}, bf16[192,1792]{1,0:T(8,128)(2,1)}) async-done(((bf16[192,1792]{1,0:T(8,128)(2,1)}, bf16[192,1792]{1,0:T(8,128)(2,1)}, bf16[192,1792]{1,0:T(8,128)(2,1)}), (bf16[192,1792]{1,0:T(8,128)(2,1)}, bf16[192,1792]{1,0:T(8,128)(2,1)}, bf16[192,1792]{1,0:T(8,128)(2,1)})) %all-reduce.7.cloned.1.call-update) | async-done | bytes 2064400 | tf_op jit(solution)/shard_map/psum | solution.py:64
  101.1 4.5 %convolution_convert_fusion.1 = bf16[1792,1024]{1,0:T(8,128)(2,1)} fusion(bf16[192,1792]{1,0:T(8,128)(2,1)} %get-tuple-element.14, bf16[192,1792]{1,0:T(8,128)(2,1)} %get-tuple-element.13, bf16[192,2048]{1,0:T(8,128)(2,1)S(1)} %all_gather.3), kind=kOutput, calls=%fused_computation.4 | convolution fusion | flops 709230592 | bytes 5439488 | tf_op jit(solution)/shard_map/dot_general | solution.py:8
  105.6 3.2 %convolution_convert_fusion.5 = bf16[1024,1792]{1,0:T(8,128)(2,1)} fusion(bf16[192,2048]{1,0:T(8,128)(2,1)S(1)} %all_gather.3, bf16[192,1792]{1,0:T(8,128)(2,1)S(1)} %copy-done.3, bf16[192,1792]{1,0:T(8,128)(2,1)S(1)} %copy-done.2, bf16[192,1792]{1,0:T(8,128)(2,1)S(1)} %copy-done.1), kind=kOutput, calls=%fused_computation.8 | convolution fusion | flops 710950912 | bytes 6127616 | tf_op jit(solution)/shard_map/dot_general | solution.py:69
  109.0 3.0 %convolution_convert_fusion.3 = bf16[1024,1792]{1,0:T(8,128)(2,1)} fusion(bf16[192,2048]{1,0:T(8,128)(2,1)S(1)} %all_gather.3, bf16[192,1792]{1,0:T(8,128)(2,1)S(1)} %copy-done.1, bf16[192,1792]{1,0:T(8,128)(2,1)S(1)} %copy-done.2), kind=kOutput, calls=%fused_computation.6 | convolution fusion | flops 709230592 | bytes 5439488 | tf_op jit(solution)/shard_map/dot_general | solution.py:72
  112.0 4.6 %fusion.12 = f32[192,1024]{1,0:T(8,128)} fusion(bf16[1024,3584]{1,0:T(8,128)(2,1)} %param.7, bf16[192,1792]{1,0:T(8,128)(2,1)S(1)} %copy-done.3, bf16[192,1792]{1,0:T(8,128)(2,1)S(1)} %copy-done.2, bf16[192,1792]{1,0:T(8,128)(2,1)S(1)} %copy-done.1), kind=kOutput, calls=%fused_computation.21 | convolution fusion | flops 709115904 | bytes 6520832 | tf_op jit(solution)/shard_map/dot_general | solution.py:14
  116.6 53.7 %all-reduce.5.cloned.1.call-done = (bf16[192,1792]{1,0:T(8,128)(2,1)}, bf16[192,1792]{1,0:T(8,128)(2,1)}, bf16[192,1792]{1,0:T(8,128)(2,1)}) async-done(((bf16[192,1792]{1,0:T(8,128)(2,1)}, bf16[192,1792]{1,0:T(8,128)(2,1)}, bf16[192,1792]{1,0:T(8,128)(2,1)}), (bf16[192,1792]{1,0:T(8,128)(2,1)}, bf16[192,1792]{1,0:T(8,128)(2,1)}, bf16[192,1792]{1,0:T(8,128)(2,1)})) %all-reduce.5.cloned.1.call-update) | async-done | bytes 2064400 | tf_op jit(solution)/shard_map/psum | solution.py:64
  170.3 3.9 %fusion.4 = f32[192,1024]{1,0:T(8,128)S(1)} fusion(bf16[1024,3584]{1,0:T(8,128)(2,1)} %param.8, bf16[192,1792]{1,0:T(8,128)(2,1)} %get-tuple-element.10, bf16[192,1792]{1,0:T(8,128)(2,1)} %get-tuple-element.11), kind=kOutput, calls=%fused_computation.13 | convolution fusion | flops 707395584 | bytes 5832704 | tf_op jit(solution)/shard_map/dot_general | solution.py:14
  174.2 3.1 %convolution_convert_fusion.2 = bf16[1024,1792]{1,0:T(8,128)(2,1)} fusion(bf16[192,2048]{1,0:T(8,128)(2,1)S(1)} %all_gather.3, bf16[192,1792]{1,0:T(8,128)(2,1)S(1)} %copy-done.4, bf16[192,1792]{1,0:T(8,128)(2,1)S(1)} %copy-done.5), kind=kOutput, calls=%fused_computation.5 | convolution fusion | flops 709230592 | bytes 5439488 | tf_op jit(solution)/shard_map/dot_general | solution.py:72
  177.4 3.2 %convolution_convert_fusion.4 = bf16[1024,1792]{1,0:T(8,128)(2,1)} fusion(bf16[192,2048]{1,0:T(8,128)(2,1)S(1)} %all_gather.3, bf16[192,1792]{1,0:T(8,128)(2,1)S(1)} %copy-done.6, bf16[192,1792]{1,0:T(8,128)(2,1)S(1)} %copy-done.5, bf16[192,1792]{1,0:T(8,128)(2,1)S(1)} %copy-done.4), kind=kOutput, calls=%fused_computation.7 | convolution fusion | flops 710950912 | bytes 6127616 | tf_op jit(solution)/shard_map/dot_general | solution.py:69
  180.6 3.1 %convolution_convert_fusion = bf16[1792,1024]{1,0:T(8,128)(2,1)} fusion(bf16[192,1792]{1,0:T(8,128)(2,1)S(1)} %copy-done.6, bf16[192,1792]{1,0:T(8,128)(2,1)S(1)} %copy-done.4, bf16[192,2048]{1,0:T(8,128)(2,1)S(1)} %all_gather.3), kind=kOutput, calls=%fused_computation.3 | convolution fusion | flops 709230592 | bytes 5439488 | tf_op jit(solution)/shard_map/dot_general | solution.py:8
  183.7 1.4 fusion.64
  185.1 0.3 slice-done.5
  185.4 2.2 %fusion.67 = bf16[192,1024]{1,0:T(8,128)(2,1)} fusion(f32[192,1024]{1,0:T(8,128)S(1)} %fusion.64, f32[192,1024]{1,0:T(8,128)S(1)} %copy-done.7, bf16[1024,3584]{1,0:T(8,128)(2,1)S(1)} %bitcast.5, bf16[192,1792]{1,0:T(8,128)(2,1)S(1)} %copy-done.1, bf16[192,1792]{1,0:T(8,128)(2,1)S(1)} %copy-done.2), kind=kOutput, calls=%fused_computation.70 | convolution fusion | flops 707985408 | bytes 7012352 | tf_op jit(solution)/shard_map/dot_general | solution.py:14
  187.6 7.2 %pad_maximum_fusion.2 = bf16[3584,1024]{1,0:T(8,128)(2,1)} fusion(bf16[1792,1024]{1,0:T(8,128)(2,1)} %convolution_convert_fusion, bf16[1792,1024]{1,0:T(8,128)(2,1)} %convolution_convert_fusion.1), kind=kLoop, calls=%fused_computation.2 | loop fusion | flops 14680064 | bytes 14680064 | tf_op jit(solution)/shard_map/concatenate | solution.py:84
  194.8 9.4 %pad_maximum_fusion = (bf16[1024,3584]{1,0:T(8,128)(2,1)}, bf16[1024,3584]{1,0:T(8,128)(2,1)}) fusion(bf16[1024,1792]{1,0:T(8,128)(2,1)} %convolution_convert_fusion.4, bf16[1024,1792]{1,0:T(8,128)(2,1)S(1)} %copy-done, bf16[1024,1792]{1,0:T(8,128)(2,1)} %convolution_convert_fusion.2, bf16[1024,1792]{1,0:T(8,128)(2,1)} %convolution_convert_fusion.3), kind=kLoop, calls=%fused_computation | loop fusion | flops 29360128 | bytes 29360128 | tf_op jit(solution)/shard_map/concatenate | solution.py:82
  204.3 3.6 %reduce-scatter.2.cloned.1.call-done = bf16[48,1024]{1,0:T(8,128)(2,1)} async-done(((bf16[192,1024]{1,0:T(8,128)(2,1)}), bf16[48,1024]{1,0:T(8,128)(2,1)}) %reduce-scatter.2.cloned.1.call-update) | async-done | bytes 98320 | tf_op jit(solution)/shard_map/reduce_scatter | solution.py:77
  (36 shorter events, 0.4 us)
Async XLA Ops:
  7.2 94.0 %all-reduce.7.cloned.1.call-start = ((), (), s32[]{:S(2)}) async-start(), calls=%async_computation.3 | async-start | bytes 4128768 | tf_op jit(solution)/shard_map/psum | solution.py:64
  8.2 29.2 %slice-start = ((s8[7340032]{0:T(1024)(128)(4,1)}), s8[4194304]{0:T(1024)(128)(4,1)S(1)}, s32[]{:S(2)}) async-start(s8[7340032]{0:T(1024)(128)(4,1)} %bitcast), calls=%async_computation.4 | async-start | bytes 8388608
  29.6 7.7 %slice-start.1 = ((s8[7340032]{0:T(1024)(128)(4,1)}), s8[3145728]{0:T(1024)(128)(4,1)S(1)}, s32[]{:S(2)}) async-start(s8[7340032]{0:T(1024)(128)(4,1)} %bitcast), calls=%async_computation.5 | async-start | bytes 6291456
  39.6 130.7 %all-reduce.5.cloned.1.call-start = ((), (), s32[]{:S(2)}) async-start(), calls=%async_computation.2 | async-start | bytes 4128768 | tf_op jit(solution)/shard_map/psum | solution.py:64
  101.1 4.5 %copy-start.1 = (bf16[192,1792]{1,0:T(8,128)(2,1)S(1)}, bf16[192,1792]{1,0:T(8,128)(2,1)}, u32[]{:S(2)}) copy-start(bf16[192,1792]{1,0:T(8,128)(2,1)} %get-tuple-element.13) | copy-start | bytes 2064388
  101.1 4.5 %copy-start.2 = (bf16[192,1792]{1,0:T(8,128)(2,1)S(1)}, bf16[192,1792]{1,0:T(8,128)(2,1)}, u32[]{:S(2)}) copy-start(bf16[192,1792]{1,0:T(8,128)(2,1)} %get-tuple-element.15) | copy-start | bytes 2064388
  101.1 4.5 %copy-start.3 = (bf16[192,1792]{1,0:T(8,128)(2,1)S(1)}, bf16[192,1792]{1,0:T(8,128)(2,1)}, u32[]{:S(2)}) copy-start(bf16[192,1792]{1,0:T(8,128)(2,1)} %get-tuple-element.14) | copy-start | bytes 2064388
  108.8 99.1 %reduce-scatter.2.cloned.1.call-start = ((), (), s32[]{:S(2)}) async-start(), calls=%async_computation.1 | async-start | bytes 491520 | tf_op jit(solution)/shard_map/reduce_scatter | solution.py:77
  170.3 3.9 %copy-start.4 = (bf16[192,1792]{1,0:T(8,128)(2,1)S(1)}, bf16[192,1792]{1,0:T(8,128)(2,1)}, u32[]{:S(2)}) copy-start(bf16[192,1792]{1,0:T(8,128)(2,1)} %get-tuple-element.10) | copy-start | bytes 2064388
  170.3 3.9 %copy-start.5 = (bf16[192,1792]{1,0:T(8,128)(2,1)S(1)}, bf16[192,1792]{1,0:T(8,128)(2,1)}, u32[]{:S(2)}) copy-start(bf16[192,1792]{1,0:T(8,128)(2,1)} %get-tuple-element.11) | copy-start | bytes 2064388
  174.2 3.1 %copy-start.6 = (bf16[192,1792]{1,0:T(8,128)(2,1)S(1)}, bf16[192,1792]{1,0:T(8,128)(2,1)}, u32[]{:S(2)}) copy-start(bf16[192,1792]{1,0:T(8,128)(2,1)} %get-tuple-element.12) | copy-start | bytes 2064388
  177.4 6.4 %slice-start.2 = ((s8[7340032]{0:T(1024)(128)(4,1)}), s8[4194304]{0:T(1024)(128)(4,1)S(1)}, s32[]{:S(2)}) async-start(s8[7340032]{0:T(1024)(128)(4,1)} %bitcast.2), calls=%async_computation.6 | async-start | bytes 8388608
  177.4 7.7 %slice-start.4 = ((s8[7340032]{0:T(1024)(128)(4,1)}), s8[4194304]{0:T(1024)(128)(4,1)S(1)}, s32[]{:S(2)}) async-start(s8[7340032]{0:T(1024)(128)(4,1)} %bitcast.4), calls=%async_computation.8 | async-start | bytes 8388608
  180.6 3.1 %slice-start.3 = ((s8[7340032]{0:T(1024)(128)(4,1)}), s8[3145728]{0:T(1024)(128)(4,1)S(1)}, s32[]{:S(2)}) async-start(s8[7340032]{0:T(1024)(128)(4,1)} %bitcast.2), calls=%async_computation.7 | async-start | bytes 6291456
  180.6 4.8 %slice-start.5 = ((s8[7340032]{0:T(1024)(128)(4,1)}), s8[3145728]{0:T(1024)(128)(4,1)S(1)}, s32[]{:S(2)}) async-start(s8[7340032]{0:T(1024)(128)(4,1)} %bitcast.4), calls=%async_computation.9 | async-start | bytes 6291456
  183.7 1.7 copy-start.7
  187.6 7.2 %copy-start = (bf16[1024,1792]{1,0:T(8,128)(2,1)S(1)}, bf16[1024,1792]{1,0:T(8,128)(2,1)}, u32[]{:S(2)}) copy-start(bf16[1024,1792]{1,0:T(8,128)(2,1)} %convolution_convert_fusion.5) | copy-start | bytes 11010052
Sparse Core Ops, SparseCore 0:
  39.7 61.3 all-reduce.6
  108.9 61.3 all-reduce.4
  187.7 20.0 reduce-scatter.1
where the time goes:
time: 215 us; the launch traced here: 214 us
  waiting for transfers between devices  106 us (49%)
  matrix products  54.4 us (25%)
  blocking collectives  21.4 us (10%)
  other arithmetic  17.6 us (8%)
  between operations  13.8 us (6%)
    psum x2, waiting for transfers between devices, body(): sums = lax.psum(parts, 'row')  103 us
    all_gather x1, blocking collectives, body(): both_all = lax.all_gather(both, 'col', axis=0, tiled=True)  21.4 us
    dot_general x6, matrix products, contract_last(): lax.dot_general(left, right, (((1,), (1,)), ((), ())), preferred_element_...  18.6 us
    concatenate x1, other arithmetic, body(): jnp.concatenate(acc_gate, axis=1)  9.45 us
    dot_general x2, matrix products, body(): jnp.dot(tok_all, uw, preferred_element_type=jnp.float32)  7.96 us
    dot_general x2, matrix products, body(): jnp.dot(tok_all, gw, preferred_element_type=jnp.float32)  7.7 us
    dot_general x2, matrix products, contract_first(): lax.dot_general(left, right, (((0,), (0,)), ((), ())), preferred_element_...  7.56 us
    concatenate x1, other arithmetic, body(): jnp.concatenate(acc_down, axis=0)  7.2 us
  transfers between devices with their start and end apart: 3, of which 3 were waited for; matrix products, arithmetic and copies ran while one was open for 17% of the time, Pallas kernels for 0%

commit v1 on v0

--- a/solution.py
+++ b/solution.py
@@ -2,6 +2,12 @@
 import jax.numpy as jnp
 from jax import lax
 from jax.sharding import PartitionSpec as P
+
+
+def laid_out(blocks, dim):
+    shape = list(blocks.shape[1:])
+    shape[dim] *= blocks.shape[0]
+    return jnp.moveaxis(blocks, 0, dim).reshape(shape)
 
 
 def contract_first(left, right):
@@ -39,7 +45,19 @@
 def body(tokens, grad_out, gate_weight, up_weight, down_weight):
     feat = tokens.shape[1]
     both = jnp.concatenate([tokens, grad_out], axis=1)
-    both_all = lax.all_gather(both, "col", axis=0, tiled=True)
+    length = lax.axis_size("col")
+    pairs = [(i, (i + 1) % length) for i in range(length)]
+    back = [(b, a) for a, b in pairs]
+    lower, upper = ([], [])
+    for hop in range(length - 1):
+        if hop % 2 == 0:
+            lower.append(lax.ppermute(lower[-1] if lower else both, "col", pairs))
+        else:
+            upper.append(lax.ppermute(upper[-1] if upper else both, "col", back))
+    tiles = jnp.stack([*lower[::-1], both, *upper])
+    shift = lax.axis_index("col") - len(lower)
+    tiles = tiles[(jnp.arange(length) - shift) % length]
+    both_all = laid_out(tiles, 0)
     tok_all = both_all[:, :feat]
     grad_all = both_all[:, feat:]
     tok_t = tok_all.T

time: 215 us -> 216 us (level)
  blocking collectives: 21.4 us -> 0 us
  waiting for transfers between devices: 106 us -> 120 us
  starting transfers between devices: 0.3 us -> 5.44 us
  local copies, waits for them, and re-layouts: 0.36 us -> 2.74 us
    all_gather x1 -> x0, blocking collectives: 21.4 us -> none  [body(): both_all = lax.all_gather(both, 'col', axis=0, tiled=True)]
    ppermute x0 -> x3, waiting for transfers between devices: none -> 13.7 us  [the longest x2 11 us: body(): lower.append(lax.ppermute(lower[-1] if lower else both, 'col', pairs))]
    ppermute x0 -> x3, starting transfers between devices: none -> 5.14 us  [the longest x2 3.05 us: body(): lower.append(lax.ppermute(lower[-1] if lower else both, 'col', pairs))]
  transfers between devices with their start and end apart: 3 -> 6, of which waited for: 3 -> 6; matrix products, arithmetic and copies ran while one was open for 17% -> 17% of each run, Pallas kernels for 0% -> 0%
where the time goes in v1:
time: 216 us
  waiting for transfers between devices  120 us (56%)
  matrix products  56.2 us (26%)
  other arithmetic  16.8 us (8%)
  between operations  13.8 us (6%)
  starting transfers between devices  5.44 us (3%)
  local copies, waits for them, and re-layouts  2.74 us (1%)
    psum x2, waiting for transfers between devices, body(): sums = lax.psum(parts, 'row')  103 us
    dot_general x6, matrix products, contract_last(): lax.dot_general(left, right, (((1,), (1,)), ((), ())), preferred_element_...  20.6 us
    ppermute x2, waiting for transfers between devices, body(): lower.append(lax.ppermute(lower[-1] if lower else both, 'col', pairs))  11 us
    concatenate x1, other arithmetic, body(): jnp.concatenate(acc_gate, axis=1)  9.45 us
    dot_general x2, matrix products, body(): jnp.dot(tok_all, uw, preferred_element_type=jnp.float32)  7.94 us
    dot_general x2, matrix products, contract_first(): lax.dot_general(left, right, (((0,), (0,)), ((), ())), preferred_element_...  7.59 us
    dot_general x2, matrix products, body(): jnp.dot(tok_all, gw, preferred_element_type=jnp.float32)  7.55 us
    concatenate x1, other arithmetic, body(): jnp.concatenate(acc_down, axis=0)  7.2 us
  transfers between devices with their start and end apart: 6, of which 6 were waited for; matrix products, arithmetic and copies ran while one was open for 17% of the time, Pallas kernels for 0%

profile of v1, /device:TPU:0, one launch (start us, length us, event | category | flops | bytes accessed | tf_op | source)
XLA Modules:
  0.0 215.5 jit_solution(11257819307568805385)
XLA Ops:
  9.0 3.1 %collective-permute-start = (bf16[48,2048]{1,0:T(8,128)(2,1)S(1)}, bf16[48,2048]{1,0:T(8,128)(2,1)S(1)}, u32[]{:S(2)}, u32[]{:S(2)}) collective-permute-start(bf16[48,2048]{1,0:T(8,128)(2,1)S(1)} %constant_dynamic-update-slice_fusion), channel_id=1, source_target_pairs={{0,1},{1,2},{2,3},{3,0},{4,5},{5,6},{6,7},{7,4},{8,9},{9,10},{10,1... | collective-permute-start | bytes 589832 | tf_op jit(solution)/shard_map/ppermute | solution.py:54
  14.1 5.7 %collective-permute-done = bf16[48,2048]{1,0:T(8,128)(2,1)S(1)} collective-permute-done((bf16[48,2048]{1,0:T(8,128)(2,1)S(1)}, bf16[48,2048]{1,0:T(8,128)(2,1)S(1)}, u32[]{:S(2)}, u32[]{:S(2)}) %collective-permute-start) | collective-permute-done | bytes 196640 | tf_op jit(solution)/shard_map/ppermute | solution.py:54
  19.9 2.7 %collective-permute-done.2 = bf16[48,2048]{1,0:T(8,128)(2,1)S(1)} collective-permute-done((bf16[48,2048]{1,0:T(8,128)(2,1)S(1)}, bf16[48,2048]{1,0:T(8,128)(2,1)S(1)}, u32[]{:S(2)}, u32[]{:S(2)}) %collective-permute-start.2) | collective-permute-done | bytes 196640 | tf_op jit(solution)/shard_map/ppermute | solution.py:56
  22.6 5.2 %collective-permute-done.1 = bf16[48,2048]{1,0:T(8,128)(2,1)S(1)} collective-permute-done((bf16[48,2048]{1,0:T(8,128)(2,1)S(1)}, bf16[48,2048]{1,0:T(8,128)(2,1)S(1)}, u32[]{:S(2)}, u32[]{:S(2)}) %collective-permute-start.1) | collective-permute-done | bytes 196640 | tf_op jit(solution)/shard_map/ppermute | solution.py:54
  28.6 3.8 %fusion.23 = bf16[192,1792]{1,0:T(8,128)(2,1)} fusion(bf16[1024,3584]{1,0:T(8,128)(2,1)} %param.7, bf16[192,2048]{1,0:T(8,128)(2,1)S(1)} %bitcast.7), kind=kOutput, calls=%fused_computation.31 | convolution fusion | flops 704987136 | bytes 4751360 | tf_op jit(solution)/shard_map/dot_general | solution.py:76
  32.4 3.8 %fusion.20 = bf16[192,1792]{1,0:T(8,128)(2,1)} fusion(bf16[1024,3584]{1,0:T(8,128)(2,1)} %param.8, bf16[192,2048]{1,0:T(8,128)(2,1)S(1)} %bitcast.8), kind=kOutput, calls=%fused_computation.30 | convolution fusion | flops 704987136 | bytes 4751360 | tf_op jit(solution)/shard_map/dot_general | solution.py:77
  36.1 4.3 %fusion.32 = bf16[192,1792]{1,0:T(8,128)(2,1)} fusion(bf16[3584,1024]{1,0:T(8,128)(2,1)} %param.9, bf16[192,2048]{1,0:T(8,128)(2,1)S(1)} %bitcast.9), kind=kOutput, calls=%fused_computation.34 | convolution fusion | flops 704987136 | bytes 4751360 | tf_op jit(solution)/shard_map/dot_general | solution.py:20
  40.5 3.8 %fusion.26 = bf16[192,1792]{1,0:T(8,128)(2,1)} fusion(bf16[1024,3584]{1,0:T(8,128)(2,1)} %param.7, bf16[192,2048]{1,0:T(8,128)(2,1)S(1)} %bitcast.10), kind=kOutput, calls=%fused_computation.32 | convolution fusion | flops 704987136 | bytes 4751360 | tf_op jit(solution)/shard_map/dot_general | solution.py:76
  44.2 4.2 %fusion.29 = bf16[192,1792]{1,0:T(8,128)(2,1)} fusion(bf16[1024,3584]{1,0:T(8,128)(2,1)} %param.8, bf16[192,2048]{1,0:T(8,128)(2,1)S(1)} %bitcast.11), kind=kOutput, calls=%fused_computation.33 | convolution fusion | flops 704987136 | bytes 4751360 | tf_op jit(solution)/shard_map/dot_general | solution.py:77
  48.4 4.3 %fusion.35 = bf16[192,1792]{1,0:T(8,128)(2,1)} fusion(bf16[3584,1024]{1,0:T(8,128)(2,1)} %param.9, bf16[192,2048]{1,0:T(8,128)(2,1)S(1)} %bitcast.12), kind=kOutput, calls=%fused_computation.35 | convolution fusion | flops 704987136 | bytes 4751360 | tf_op jit(solution)/shard_map/dot_general | solution.py:20
  52.7 49.6 %all-reduce.7.cloned.1.call-done = (bf16[192,1792]{1,0:T(8,128)(2,1)}, bf16[192,1792]{1,0:T(8,128)(2,1)}, bf16[192,1792]{1,0:T(8,128)(2,1)}) async-done(((bf16[192,1792]{1,0:T(8,128)(2,1)}, bf16[192,1792]{1,0:T(8,128)(2,1)}, bf16[192,1792]{1,0:T(8,128)(2,1)}), (bf16[192,1792]{1,0:T(8,128)(2,1)}, bf16[192,1792]{1,0:T(8,128)(2,1)}, bf16[192,1792]{1,0:T(8,128)(2,1)})) %all-reduce.7.cloned.1.call-update) | async-done | bytes 2064400 | tf_op jit(solution)/shard_map/psum | solution.py:82
  102.3 4.5 %convolution_convert_fusion.1 = bf16[1792,1024]{1,0:T(8,128)(2,1)} fusion(bf16[192,1792]{1,0:T(8,128)(2,1)} %get-tuple-element.14, bf16[192,1792]{1,0:T(8,128)(2,1)} %get-tuple-element.13, bf16[192,2048]{1,0:T(8,128)(2,1)S(1)} %bitcast.13), kind=kOutput, calls=%fused_computation.5 | convolution fusion | flops 709230592 | bytes 5439488 | tf_op jit(solution)/shard_map/dot_general | solution.py:14
  106.8 3.2 %convolution_convert_fusion.5 = bf16[1024,1792]{1,0:T(8,128)(2,1)} fusion(bf16[192,2048]{1,0:T(8,128)(2,1)S(1)} %bitcast.14, bf16[192,1792]{1,0:T(8,128)(2,1)S(1)} %copy-done.3, bf16[192,1792]{1,0:T(8,128)(2,1)S(1)} %copy-done.2, bf16[192,1792]{1,0:T(8,128)(2,1)S(1)} %copy-done.1), kind=kOutput, calls=%fused_computation.9 | convolution fusion | flops 710950912 | bytes 6127616 | tf_op jit(solution)/shard_map/dot_general | solution.py:87
  110.2 3.0 %convolution_convert_fusion.3 = bf16[1024,1792]{1,0:T(8,128)(2,1)} fusion(bf16[192,2048]{1,0:T(8,128)(2,1)S(1)} %bitcast.15, bf16[192,1792]{1,0:T(8,128)(2,1)S(1)} %copy-done.1, bf16[192,1792]{1,0:T(8,128)(2,1)S(1)} %copy-done.2), kind=kOutput, calls=%fused_computation.7 | convolution fusion | flops 709230592 | bytes 5439488 | tf_op jit(solution)/shard_map/dot_general | solution.py:90
  113.2 4.6 %fusion.12 = f32[192,1024]{1,0:T(8,128)} fusion(bf16[1024,3584]{1,0:T(8,128)(2,1)} %param.7, bf16[192,1792]{1,0:T(8,128)(2,1)S(1)} %copy-done.3, bf16[192,1792]{1,0:T(8,128)(2,1)S(1)} %copy-done.2, bf16[192,1792]{1,0:T(8,128)(2,1)S(1)} %copy-done.1), kind=kOutput, calls=%fused_computation.22 | convolution fusion | flops 709115904 | bytes 6520832 | tf_op jit(solution)/shard_map/dot_general | solution.py:20
  117.8 53.6 %all-reduce.5.cloned.1.call-done = (bf16[192,1792]{1,0:T(8,128)(2,1)}, bf16[192,1792]{1,0:T(8,128)(2,1)}, bf16[192,1792]{1,0:T(8,128)(2,1)}) async-done(((bf16[192,1792]{1,0:T(8,128)(2,1)}, bf16[192,1792]{1,0:T(8,128)(2,1)}, bf16[192,1792]{1,0:T(8,128)(2,1)}), (bf16[192,1792]{1,0:T(8,128)(2,1)}, bf16[192,1792]{1,0:T(8,128)(2,1)}, bf16[192,1792]{1,0:T(8,128)(2,1)})) %all-reduce.5.cloned.1.call-update) | async-done | bytes 2064400 | tf_op jit(solution)/shard_map/psum | solution.py:82
  171.5 3.9 %fusion.4 = f32[192,1024]{1,0:T(8,128)S(1)} fusion(bf16[1024,3584]{1,0:T(8,128)(2,1)} %param.8, bf16[192,1792]{1,0:T(8,128)(2,1)} %get-tuple-element.10, bf16[192,1792]{1,0:T(8,128)(2,1)} %get-tuple-element.11), kind=kOutput, calls=%fused_computation.14 | convolution fusion | flops 707395584 | bytes 5832704 | tf_op jit(solution)/shard_map/dot_general | solution.py:20
  175.4 3.1 %convolution_convert_fusion.2 = bf16[1024,1792]{1,0:T(8,128)(2,1)} fusion(bf16[192,2048]{1,0:T(8,128)(2,1)S(1)} %bitcast.16, bf16[192,1792]{1,0:T(8,128)(2,1)S(1)} %copy-done.4, bf16[192,1792]{1,0:T(8,128)(2,1)S(1)} %copy-done.5), kind=kOutput, calls=%fused_computation.6 | convolution fusion | flops 709230592 | bytes 5439488 | tf_op jit(solution)/shard_map/dot_general | solution.py:90
  178.5 3.2 %convolution_convert_fusion.4 = bf16[1024,1792]{1,0:T(8,128)(2,1)} fusion(bf16[192,2048]{1,0:T(8,128)(2,1)S(1)} %bitcast.17, bf16[192,1792]{1,0:T(8,128)(2,1)S(1)} %copy-done.6, bf16[192,1792]{1,0:T(8,128)(2,1)S(1)} %copy-done.5, bf16[192,1792]{1,0:T(8,128)(2,1)S(1)} %copy-done.4), kind=kOutput, calls=%fused_computation.8 | convolution fusion | flops 710950912 | bytes 6127616 | tf_op jit(solution)/shard_map/dot_general | solution.py:87
  181.8 3.1 %convolution_convert_fusion = bf16[1792,1024]{1,0:T(8,128)(2,1)} fusion(bf16[192,1792]{1,0:T(8,128)(2,1)S(1)} %copy-done.6, bf16[192,1792]{1,0:T(8,128)(2,1)S(1)} %copy-done.4, bf16[192,2048]{1,0:T(8,128)(2,1)S(1)} %bitcast.18), kind=kOutput, calls=%fused_computation.4 | convolution fusion | flops 709230592 | bytes 5439488 | tf_op jit(solution)/shard_map/dot_general | solution.py:14
  186.6 2.2 %fusion.67 = bf16[192,1024]{1,0:T(8,128)(2,1)} fusion(f32[192,1024]{1,0:T(8,128)S(1)} %fusion.64, f32[192,1024]{1,0:T(8,128)S(1)} %copy-done.7, bf16[1024,3584]{1,0:T(8,128)(2,1)S(1)} %bitcast.26, bf16[192,1792]{1,0:T(8,128)(2,1)S(1)} %copy-done.1, bf16[192,1792]{1,0:T(8,128)(2,1)S(1)} %copy-done.2), kind=kOutput, calls=%fused_computation.71 | convolution fusion | flops 707985408 | bytes 7012352 | tf_op jit(solution)/shard_map/dot_general | solution.py:20
  188.8 7.2 %pad_maximum_fusion.2 = bf16[3584,1024]{1,0:T(8,128)(2,1)} fusion(bf16[1792,1024]{1,0:T(8,128)(2,1)} %convolution_convert_fusion, bf16[1792,1024]{1,0:T(8,128)(2,1)} %convolution_convert_fusion.1), kind=kLoop, calls=%fused_computation.3 | loop fusion | flops 14680064 | bytes 14680064 | tf_op jit(solution)/shard_map/concatenate | solution.py:102
  196.0 9.5 %pad_maximum_fusion = (bf16[1024,3584]{1,0:T(8,128)(2,1)}, bf16[1024,3584]{1,0:T(8,128)(2,1)}) fusion(bf16[1024,1792]{1,0:T(8,128)(2,1)} %convolution_convert_fusion.4, bf16[1024,1792]{1,0:T(8,128)(2,1)S(1)} %copy-done, bf16[1024,1792]{1,0:T(8,128)(2,1)} %convolution_convert_fusion.2, bf16[1024,1792]{1,0:T(8,128)(2,1)} %convolution_convert_fusion.3), kind=kLoop, calls=%fused_computation.1 | loop fusion | flops 29360128 | bytes 29360128 | tf_op jit(solution)/shard_map/concatenate | solution.py:100
  205.4 3.5 %reduce-scatter.2.cloned.1.call-done = bf16[48,1024]{1,0:T(8,128)(2,1)} async-done(((bf16[192,1024]{1,0:T(8,128)(2,1)}), bf16[48,1024]{1,0:T(8,128)(2,1)}) %reduce-scatter.2.cloned.1.call-update) | async-done | bytes 98320 | tf_op jit(solution)/shard_map/reduce_scatter | solution.py:95
  (41 shorter events, 6.7 us)
Async XLA Ops:
  7.2 95.1 %all-reduce.7.cloned.1.call-start = ((), (), s32[]{:S(2)}) async-start(), calls=%async_computation.3 | async-start | bytes 4128768 | tf_op jit(solution)/shard_map/psum | solution.py:82
  9.0 10.9 %collective-permute-start = (bf16[48,2048]{1,0:T(8,128)(2,1)S(1)}, bf16[48,2048]{1,0:T(8,128)(2,1)S(1)}, u32[]{:S(2)}, u32[]{:S(2)}) collective-permute-start(bf16[48,2048]{1,0:T(8,128)(2,1)S(1)} %constant_dynamic-update-slice_fusion), channel_id=1, source_target_pairs={{0,1},{1,2},{2,3},{3,0},{4,5},{5,6},{6,7},{7,4},{8,9},{9,10},{10,1... | collective-permute-start | bytes 589832 | tf_op jit(solution)/shard_map/ppermute | solution.py:54
  12.1 10.6 %collective-permute-start.2 = (bf16[48,2048]{1,0:T(8,128)(2,1)S(1)}, bf16[48,2048]{1,0:T(8,128)(2,1)S(1)}, u32[]{:S(2)}, u32[]{:S(2)}) collective-permute-start(bf16[48,2048]{1,0:T(8,128)(2,1)S(1)} %constant_dynamic-update-slice_fusion), channel_id=1, source_target_pairs={{1,0},{2,1},{3,2},{0,3},{5,4},{6,5},{7,6},{4,7},{9,8},{10,9},{11,1... | collective-permute-start | bytes 589832 | tf_op jit(solution)/shard_map/ppermute | solution.py:56
  19.9 8.0 %collective-permute-start.1 = (bf16[48,2048]{1,0:T(8,128)(2,1)S(1)}, bf16[48,2048]{1,0:T(8,128)(2,1)S(1)}, u32[]{:S(2)}, u32[]{:S(2)}) collective-permute-start(bf16[48,2048]{1,0:T(8,128)(2,1)S(1)} %collective-permute-done), channel_id=1, source_target_pairs={{0,1},{1,2},{2,3},{3,0},{4,5},{5,6},{6,7},{7,4},{8,9},{9,10},{10,1... | collective-permute-start | bytes 589832 | tf_op jit(solution)/shard_map/ppermute | solution.py:54
  40.4 131.0 %all-reduce.5.cloned.1.call-start = ((), (), s32[]{:S(2)}) async-start(), calls=%async_computation.2 | async-start | bytes 4128768 | tf_op jit(solution)/shard_map/psum | solution.py:82
  102.3 4.5 %copy-start.1 = (bf16[192,1792]{1,0:T(8,128)(2,1)S(1)}, bf16[192,1792]{1,0:T(8,128)(2,1)}, u32[]{:S(2)}) copy-start(bf16[192,1792]{1,0:T(8,128)(2,1)} %get-tuple-element.13) | copy-start | bytes 2064388
  102.3 4.5 %copy-start.2 = (bf16[192,1792]{1,0:T(8,128)(2,1)S(1)}, bf16[192,1792]{1,0:T(8,128)(2,1)}, u32[]{:S(2)}) copy-start(bf16[192,1792]{1,0:T(8,128)(2,1)} %get-tuple-element.15) | copy-start | bytes 2064388
  102.3 4.5 %copy-start.3 = (bf16[192,1792]{1,0:T(8,128)(2,1)S(1)}, bf16[192,1792]{1,0:T(8,128)(2,1)}, u32[]{:S(2)}) copy-start(bf16[192,1792]{1,0:T(8,128)(2,1)} %get-tuple-element.14) | copy-start | bytes 2064388
  109.9 99.0 %reduce-scatter.2.cloned.1.call-start = ((), (), s32[]{:S(2)}) async-start(), calls=%async_computation.1 | async-start | bytes 491520 | tf_op jit(solution)/shard_map/reduce_scatter | solution.py:95
  171.5 3.9 %copy-start.4 = (bf16[192,1792]{1,0:T(8,128)(2,1)S(1)}, bf16[192,1792]{1,0:T(8,128)(2,1)}, u32[]{:S(2)}) copy-start(bf16[192,1792]{1,0:T(8,128)(2,1)} %get-tuple-element.10) | copy-start | bytes 2064388
  171.5 3.9 %copy-start.5 = (bf16[192,1792]{1,0:T(8,128)(2,1)S(1)}, bf16[192,1792]{1,0:T(8,128)(2,1)}, u32[]{:S(2)}) copy-start(bf16[192,1792]{1,0:T(8,128)(2,1)} %get-tuple-element.11) | copy-start | bytes 2064388
  175.4 3.1 %copy-start.6 = (bf16[192,1792]{1,0:T(8,128)(2,1)S(1)}, bf16[192,1792]{1,0:T(8,128)(2,1)}, u32[]{:S(2)}) copy-start(bf16[192,1792]{1,0:T(8,128)(2,1)} %get-tuple-element.12) | copy-start | bytes 2064388
  178.5 6.4 %slice-start = ((s8[7340032]{0:T(1024)(128)(4,1)}), s8[4194304]{0:T(1024)(128)(4,1)S(1)}, s32[]{:S(2)}) async-start(s8[7340032]{0:T(1024)(128)(4,1)} %bitcast.23), calls=%async_computation.4 | async-start | bytes 8388608
  178.5 7.7 %slice-start.2 = ((s8[7340032]{0:T(1024)(128)(4,1)}), s8[4194304]{0:T(1024)(128)(4,1)S(1)}, s32[]{:S(2)}) async-start(s8[7340032]{0:T(1024)(128)(4,1)} %bitcast.25), calls=%async_computation.6 | async-start | bytes 8388608
  181.8 3.1 %slice-start.1 = ((s8[7340032]{0:T(1024)(128)(4,1)}), s8[3145728]{0:T(1024)(128)(4,1)S(1)}, s32[]{:S(2)}) async-start(s8[7340032]{0:T(1024)(128)(4,1)} %bitcast.23), calls=%async_computation.5 | async-start | bytes 6291456
  181.8 4.8 %slice-start.3 = ((s8[7340032]{0:T(1024)(128)(4,1)}), s8[3145728]{0:T(1024)(128)(4,1)S(1)}, s32[]{:S(2)}) async-start(s8[7340032]{0:T(1024)(128)(4,1)} %bitcast.25), calls=%async_computation.7 | async-start | bytes 6291456
  184.9 1.7 copy-start.7
  188.8 7.2 %copy-start = (bf16[1024,1792]{1,0:T(8,128)(2,1)S(1)}, bf16[1024,1792]{1,0:T(8,128)(2,1)}, u32[]{:S(2)}) copy-start(bf16[1024,1792]{1,0:T(8,128)(2,1)} %convolution_convert_fusion.5) | copy-start | bytes 11010052
Sparse Core Ops, SparseCore 0:
  40.5 61.6 all-reduce.6
  110.1 61.3 all-reduce.4
  188.9 20.0 reduce-scatter.1
